TPU v7x, 512 devices: a whole 4x8x8 slice. The times are simulated.
512 devices in a mesh: blk: 64 (over z_hi, y, core), seq: 4 (over x), mp: 2 (over z_lo).
Axes of the slice: x: 4, y: 8, z: 8 (z_hi: 4, z_lo: 2; z = z_hi * 2 + z_lo), core: 2. Of those that a mesh axis runs over, the one named last changes fastest.
Arguments:
- hidden: bfloat16 [8, 512, 1536], P(('mp', 'seq'), 'blk'), parts along dimension 0, may hold values from -6 to 6
- labels: int32 [4, 512], P('seq'), may hold values from 0 to 50303
- lengths: int32 [4, 8], P('seq'), may hold values from 1 to 256, 512 in all within a row
- owners: int32 [32], replicated, may hold values from 0 to 31, each once
- w_inner: bfloat16 [3072, 2, 3072], P('mp', None, 'blk'), parts along dimension 0, may hold values from -0.15625 to 0.15625
- w_bcdt: bfloat16 [3072, 304], P('mp'), parts along dimension 0, may hold values from -0.15625 to 0.15625
- conv_inner: float32 [8, 3072], P('mp', 'blk'), parts along dimension 0, may hold values from -3 to 3
- conv_bc: float32 [8, 256], P('mp'), parts along dimension 0, may hold values from -3 to 3
- dt_bias: float32 [96], P('mp'), parts along dimension 0, may hold values from -3 to 0.5
- decay_rate: float32 [96], P('mp'), parts along dimension 0, may hold values from 0.01 to 1
- d_skip: float32 [96], P('mp'), parts along dimension 0, may hold values from 0.5 to 2
- norm_gain: float32 [6144], P(('mp', 'blk')), parts along dimension 0, may hold values from 0.5 to 1.5
- w_out: bfloat16 [6144, 1536], P(('mp', 'blk')), parts along dimension 0, may hold values from -0.109375 to 0.109375
- final_gain: float32 [3072], P('mp'), parts along dimension 0, may hold values from 0.5 to 1.5
- w_head: bfloat16 [3072, 50304], P('mp', 'blk'), parts along dimension 0, may hold values from -0.33170174 to 0.33170174
Outputs:
- layer_out: bfloat16 [8, 512, 1536], P(('mp', 'seq'), 'blk'), parts along dimension 0
- token_logprob: float32 [8, 512], P(('mp', 'seq'), 'blk'), parts along dimension 0
- seq_logprob: float32 [64], P(('mp', 'seq')), parts along dimension 0
There are 2 independent parts, one for each index of `mp`. A program takes and returns all parts, laid end to end along the dimension named above; an argument that names none is the same for every part. Nothing has to cross between parts.
Inputs may be any that keep to these rules, and one draw needn't show every extreme that they name: The 8 lengths of a group sum to 512 and the longest is exactly 256. `owners`: every output slot is named once.
All inputs are finite; a program needn't handle non-finite values.
Results may differ from a plain program's by a relative error of at most 0.0055.
Values may be sent and summed in bfloat16 or wider, within the bound.
No kernel may reach another device: no remote copies, remote signals or barrier semaphores. Data moves between devices by JAX's collectives and lax.ppermute only.
A program may use at most 64 MiB of HBM per device.

v0:
```python
import jax
import jax.numpy as jnp
from jax import lax
from jax.sharding import PartitionSpec as P

D = 1536
HEADDIM = 64
NSTATE = 128
SCAN_BLOCK = 256
CONV = 4
EPSILON = 1e-05
HIGH = lax.Precision.HIGHEST


def segments_of(lengths, count):
    starts = jnp.cumsum(lengths, axis=-1) - lengths
    places = jnp.arange(count, dtype=jnp.int32)
    segment = jnp.sum((places[:, None] >= starts[None, :]).astype(jnp.int32), axis=-1) - 1
    first = jnp.take(starts, segment)
    return (segment, places - first)


def causal_conv(values, weights, position):
    total = values * weights[0]
    for shift_by in range(1, CONV):
        moved = jnp.concatenate(
            [jnp.zeros_like(values[:shift_by, :]), values[:-shift_by, :]], axis=0
        )
        total = (
            total + moved * weights[shift_by] * (position >= shift_by).astype(jnp.float32)[:, None]
        )
    return total


def final_norm(values, gain):
    widened = values.astype(jnp.float32)
    scale = lax.rsqrt(jnp.mean(widened * widened, axis=-1, keepdims=True) + EPSILON)
    return (widened * scale * gain).astype(jnp.bfloat16)


def shards(
    hidden,
    labels,
    lengths,
    owners,
    w_inner,
    w_bcdt,
    conv_inner,
    conv_bc,
    dt_bias,
    decay_rate,
    d_skip,
    norm_gain,
    w_out,
    final_gain,
    w_head,
):
    rows_own = hidden[0]
    rows_count = rows_own.shape[0]
    blk_count = lax.axis_size("blk")
    blk_index = lax.axis_index("blk")
    gathered = lax.all_gather(rows_own, "blk", axis=0, tiled=True)
    tokens_all = gathered.shape[0]
    channels = w_inner.shape[2]
    inner_total = channels * blk_count
    inner_proj = jnp.dot(
        gathered, w_inner.reshape(D, 2 * channels), preferred_element_type=jnp.float32
    ).astype(jnp.bfloat16)
    state_proj = jnp.dot(gathered, w_bcdt, preferred_element_type=jnp.float32).astype(jnp.bfloat16)
    gate_half = inner_proj[:, :channels].astype(jnp.float32)
    segment, position = segments_of(lengths[0], tokens_all)
    conv_value = jax.nn.silu(
        causal_conv(inner_proj[:, channels:].astype(jnp.float32), conv_inner, position)
    )
    conv_state = jax.nn.silu(
        causal_conv(state_proj[:, : 2 * NSTATE].astype(jnp.float32), conv_bc, position)
    )
    input_map = conv_state[:, :NSTATE]
    output_map = conv_state[:, NSTATE:]
    step_size = jax.nn.softplus(state_proj[:, 2 * NSTATE :].astype(jnp.float32) + dt_bias)
    log_heads = -(step_size * decay_rate)
    first_channel = blk_index * channels
    channel_head = (first_channel + jnp.arange(channels, dtype=jnp.int32)) // HEADDIM
    head_low = first_channel // HEADDIM
    head_high = (first_channel + channels - 1) // HEADDIM
    mask_high = (channel_head == head_high).astype(jnp.float32)
    mask_low = 1.0 - mask_high
    step_pair = jnp.concatenate(
        [
            lax.dynamic_slice_in_dim(step_size, head_low, 1, 1),
            lax.dynamic_slice_in_dim(step_size, head_high, 1, 1),
        ],
        axis=1,
    )
    log_pair = jnp.concatenate(
        [
            lax.dynamic_slice_in_dim(log_heads, head_low, 1, 1),
            lax.dynamic_slice_in_dim(log_heads, head_high, 1, 1),
        ],
        axis=1,
    )
    step_channel = step_pair[:, 0:1] * mask_low + step_pair[:, 1:2] * mask_high
    driven = conv_value * step_channel
    slot_masks = (mask_low, mask_high)
    blocks = tokens_all // SCAN_BLOCK
    order = jnp.arange(SCAN_BLOCK, dtype=jnp.int32)
    causal = order[:, None] >= order[None, :]

    def block_step(carry, inputs):
        carried, previous = carry
        drive_block, in_block, out_block, log_block, seg_block = inputs
        cumulative = jnp.cumsum(log_block, axis=0)
        gram = jnp.dot(out_block, in_block.T, precision=HIGH)
        same = (seg_block[:, None] == seg_block[None, :]) & causal
        result = jnp.zeros((SCAN_BLOCK, channels), jnp.float32)
        for slot_index in range(2):
            column = cumulative[:, slot_index]
            spread = jnp.minimum(column[:, None] - column[None, :], 0.0)
            weights = jnp.where(same, jnp.exp(spread), 0.0)
            result = result + jnp.dot(
                gram * weights, drive_block * slot_masks[slot_index], precision=HIGH
            )
        carried_in = carried * (seg_block[0] == previous).astype(jnp.float32)
        rising = jnp.exp(cumulative[:, 0:1]) * mask_low + jnp.exp(cumulative[:, 1:2]) * mask_high
        leading = (seg_block == seg_block[0]).astype(jnp.float32)[:, None]
        result = result + leading * rising * jnp.dot(out_block, carried_in.T, precision=HIGH)
        trailing = (seg_block == seg_block[-1]).astype(jnp.float32)[:, None]
        tail_low = jnp.exp(cumulative[-1:, 0:1] - cumulative[:, 0:1])
        tail_high = jnp.exp(cumulative[-1:, 1:2] - cumulative[:, 1:2])
        tail = tail_low * mask_low + tail_high * mask_high
        whole_block = (seg_block[-1] == seg_block[0]).astype(jnp.float32)
        carried_new = whole_block * rising[-1][:, None] * carried_in + jnp.dot(
            (drive_block * tail * trailing).T, in_block, precision=HIGH
        )
        return ((carried_new, seg_block[-1]), result)

    initial = (jnp.zeros((channels, NSTATE), jnp.float32), jnp.int32(-1))
    scan_inputs = (
        driven.reshape(blocks, SCAN_BLOCK, channels),
        input_map.reshape(blocks, SCAN_BLOCK, NSTATE),
        output_map.reshape(blocks, SCAN_BLOCK, NSTATE),
        log_pair.reshape(blocks, SCAN_BLOCK, 2),
        segment.reshape(blocks, SCAN_BLOCK),
    )
    final_carry, scanned = lax.scan(block_step, initial, scan_inputs)
    mixed = scanned.reshape(tokens_all, channels) + jnp.take(d_skip, channel_head) * conv_value
    gated = mixed * jax.nn.silu(gate_half)
    squares = lax.psum(jnp.sum(gated * gated, axis=1), "blk")
    inverse = lax.rsqrt(squares / inner_total + EPSILON)
    gated_norm = (gated * inverse[:, None] * norm_gain).astype(jnp.bfloat16)
    delta_own = lax.psum_scatter(
        jnp.dot(gated_norm, w_out, preferred_element_type=jnp.float32),
        "blk",
        scatter_dimension=0,
        tiled=True,
    )
    layer_own = (rows_own.astype(jnp.float32) + delta_own).astype(jnp.bfloat16)
    logits = jnp.dot(
        lax.all_gather(final_norm(layer_own, final_gain), "blk", axis=0, tiled=True),
        w_head,
        preferred_element_type=jnp.float32,
    )
    vocab_local = w_head.shape[1]
    local_label = labels[0] - blk_index * vocab_local
    hit = jnp.arange(vocab_local, dtype=jnp.int32)[None, :] == local_label[:, None]
    target_local = jnp.sum(jnp.where(hit, logits, 0.0), axis=1)
    top_local = jnp.max(logits, axis=1)
    top_all = lax.pmax(top_local, "blk")
    expsum_local = jnp.sum(jnp.exp(logits - top_all[:, None]), axis=1)
    expsum_all, target_all = lax.psum((expsum_local, target_local), "blk")
    logprob = target_all - (top_all + jnp.log(expsum_all))
    token_own = lax.dynamic_slice_in_dim(logprob, blk_index * rows_count, rows_count, 0)
    seqs_count = lengths.shape[1]
    onehot = (segment[:, None] == jnp.arange(seqs_count, dtype=jnp.int32)[None, :]).astype(
        jnp.float32
    )
    sums = jnp.dot(logprob, onehot, precision=HIGH)
    seq_index = lax.axis_index("seq")
    mine = lax.dynamic_slice_in_dim(owners, seq_index * seqs_count, seqs_count, 0)
    placement = (mine[:, None] == jnp.arange(owners.shape[0], dtype=jnp.int32)[None, :]).astype(
        jnp.float32
    )
    spread_sums = jnp.dot(sums, placement, precision=HIGH)
    seq_own = lax.psum_scatter(spread_sums, "seq", scatter_dimension=0, tiled=True)
    return (layer_own[None], token_own[None], seq_own)


def solution(mesh):
    in_specs = (
        P(("mp", "seq"), "blk", None),
        P("seq", None),
        P("seq", None),
        P(),
        P("mp", None, "blk"),
        P("mp", None),
        P("mp", "blk"),
        P("mp", None),
        P("mp"),
        P("mp"),
        P("mp"),
        P(("mp", "blk")),
        P(("mp", "blk"), None),
        P("mp"),
        P("mp", "blk"),
    )
    out_specs = (P(("mp", "seq"), "blk", None), P(("mp", "seq"), "blk"), P(("mp", "seq")))
    return jax.shard_map(shards, mesh=mesh, in_specs=in_specs, out_specs=out_specs, check_vma=False)
```

profile of v0, /device:TPU:1, one launch (start us, length us, event | category | flops | bytes accessed | tf_op | source)
XLA Modules:
  0.0 819.6 jit_solution(5413940078656478816)
XLA Ops:
  10.2 1.4 gather_fusion
  13.6 1.4 slice_bitcast_fusion.3
  15.0 4.4 compare_select_fusion.5
  21.0 80.3 %all-gather.6.cloned.1.call-done = bf16[1,512,1536]{2,1,0:T(8,128)(2,1)} async-done(((bf16[1,8,1536]{2,1,0:T(8,128)(2,1)}), bf16[1,512,1536]{2,1,0:T(8,128)(2,1)}) %all-gather.6.cloned.1.call-update) | async-done | bytes 1572880 | tf_op jit(solution)/shard_map/all_gather | solution.py:62
  101.3 2.3 fusion.71
  104.8 2.0 fusion.74
  108.1 29.1 %while.17 = (s32[]{:T(128)}, f32[48,128]{1,0:T(8,128)S(1)}, s32[]{:T(128)}, f32[2,256,48]{1,0,2:T(2,128)}, s32[2,256]{1,0:T(2,128)}, /*index=5*/f32[2,256,2]{1,2...) while((s32[]{:T(128)}, f32[48,128]{1,0:T(8,128)S(1)}, ...), condition=%wide.region_5.6_spmd.clone.clone.clone, body=%wide.region_2.5_spmd.clone.clone.clone.sunk | while | flops 215140816 | bytes 2177448 | solution.py:145
  113.8 1.3 constant_dynamic-slice_fusion.12
  115.1 1.9 compare_convert_fusion.10
  118.0 2.2 dynamic_update_slice.8
  125.0 1.3 fusion.130
  128.4 1.3 constant_dynamic-slice_fusion.12
  129.6 1.9 compare_convert_fusion.10
  132.5 2.2 dynamic_update_slice.8
  138.8 138.1 %psum.21 = f32[512]{0:T(512)S(1)} all-reduce(f32[512]{0:T(512)S(1)} %get-tuple-element.251), channel_id=1, replica_groups=mesh['blk'=64,'seq'=4,'mp'=2] {'blk'}, use_global_device_ids=true, to_apply=%region_7.8 | all-reduce | flops 512 | bytes 4096 | tf_op jit(solution)/shard_map/psum | solution.py:148
  276.9 3.0 fusion.85
  279.9 148.0 %reduce-scatter.2.cloned.1.call-done = f32[8,1536]{1,0:T(8,128)} async-done(((f32[512,1536]{1,0:T(8,128)}), f32[8,1536]{1,0:T(8,128)}) %reduce-scatter.2.cloned.1.call-update) | async-done | bytes 49168 | tf_op jit(solution)/shard_map/reduce_scatter | solution.py:151
  429.7 1.3 dynamic-slice
  431.7 85.4 %all-gather.4.cloned.1.call-done = bf16[512,1536]{1,0:T(8,128)(2,1)} async-done(((bf16[8,1536]{1,0:T(8,128)(2,1)}), bf16[512,1536]{1,0:T(8,128)(2,1)}) %all-gather.4.cloned.1.call-update) | async-done | bytes 1572880 | tf_op jit(solution)/shard_map/all_gather | solution.py:159
  517.1 4.0 fusion.101
  521.1 138.1 %pmax.7 = f32[512]{0:T(512)S(1)} all-reduce(f32[512]{0:T(512)S(1)} %get-tuple-element.299), channel_id=1, replica_groups=mesh['blk'=64,'seq'=4,'mp'=2] {'blk'}, use_global_device_ids=true, to_apply=%region_13.14 | all-reduce | flops 512 | bytes 4096 | tf_op jit(solution)/shard_map/pmax | solution.py:168
  659.2 1.9 exponential_reduce_fusion
  661.1 142.0 %all-reduce.7 = (f32[512]{0:T(512)S(1)}, f32[512]{0:T(512)S(1)}) all-reduce(f32[512]{0:T(512)S(1)} %get-tuple-element.222, f32[512]{0:T(512)S(1)} %get-tuple-element.221), channel_id=1, replica_groups=mesh['blk'=64,'seq'=4,'mp'=2] {'blk'}, use_global_device_ids=true, to_apply=%region_11.12 | all-reduce | flops 1024 | bytes 8192 | tf_op jit(solution)/shard_map/psum | solution.py:170
  803.6 8.4 %all-reduce.6 = f32[32]{0:T(128)S(1)} all-reduce(f32[32]{0:T(128)S(1)} %convolution_bitcast_fusion.1), channel_id=4, replica_groups=mesh['blk'=64,'seq'=4,'mp'=2] {'seq'}, use_global_device_ids=true, to_apply=%region_16.17.clone | all-reduce | flops 32 | bytes 256
  (135 shorter events, 25.4 us)
Async XLA Ops:
  7.2 509.9 %copy-start = (bf16[1536,786]{0,1:T(8,128)(2,1)S(1)}, bf16[1536,786]{0,1:T(8,128)(2,1)}, u32[]{:S(2)}) copy-start(bf16[1536,786]{0,1:T(8,128)(2,1)} %param.31) | copy-start | bytes 7243780
  7.2 94.1 %all-gather.6.cloned.1.call-start = ((), (), s32[]{:S(2)}) async-start(), calls=%async_computation.3 | async-start | bytes 1597440 | tf_op jit(solution)/shard_map/all_gather | solution.py:62
  7.9 420.1 %reduce-scatter.2.cloned.1.call-start = ((), (), s32[]{:S(2)}) async-start(), calls=%async_computation.1 | async-start | bytes 3194880 | tf_op jit(solution)/shard_map/reduce_scatter | solution.py:151
  9.6 94.1 %copy-start.5 = (s32[512]{0:T(512)}, s32[512]{0:T(512)S(1)}, u32[]{:S(2)}) copy-start(s32[512]{0:T(512)S(1)} %get-tuple-element.290) | copy-start | bytes 6148
  20.1 83.6 %copy-start.11 = (f32[512]{0:T(512)}, f32[512]{0:T(512)S(1)}, u32[]{:S(2)}) copy-start(f32[512]{0:T(512)S(1)} %get-tuple-element.257) | copy-start | bytes 6148
  20.1 83.6 %copy-start.7 = (f32[512]{0:T(512)}, f32[512]{0:T(512)S(1)}, u32[]{:S(2)}) copy-start(f32[512]{0:T(512)S(1)} %get-tuple-element.287) | copy-start | bytes 6148
  20.1 83.6 %copy-start.9 = (f32[512]{0:T(512)}, f32[512]{0:T(512)S(1)}, u32[]{:S(2)}) copy-start(f32[512]{0:T(512)S(1)} %get-tuple-element.288) | copy-start | bytes 6148
  104.7 2.3 copy-start.8
  104.7 2.3 copy-start.10
  104.8 2.3 copy-start.12
  104.8 2.3 copy-start.15
  104.8 2.3 copy-start.16
  104.8 2.3 copy-start.17
  104.8 2.3 copy-start.18
  104.8 2.3 copy-start.19
  104.8 2.3 copy-start.20
  108.1 168.8 %copy-start.1 = (bf16[48,1536]{1,0:T(8,128)(2,1)S(1)}, bf16[48,1536]{1,0:T(8,128)(2,1)}, u32[]{:S(2)}) copy-start(bf16[48,1536]{1,0:T(8,128)(2,1)} %param.29) | copy-start | bytes 442372
  279.9 148.1 %copy-start.4 = (bf16[1,8,1536]{2,1,0:T(8,128)(2,1)S(1)}, bf16[1,8,1536]{2,1,0:T(8,128)(2,1)}, u32[]{:S(2)}) copy-start(bf16[1,8,1536]{2,1,0:T(8,128)(2,1)} %param.17) | copy-start | bytes 73732
  279.9 149.1 %copy-start.13 = (f32[1536]{0:T(1024)S(1)}, f32[1536]{0:T(1024)}, u32[]{:S(2)}) copy-start(f32[1536]{0:T(1024)} %param.30) | copy-start | bytes 18436
  279.9 149.8 %copy-start.23 = (s32[32]{0:T(128)S(1)}, s32[32]{0:T(128)}, u32[]{:S(2)}) copy-start(s32[32]{0:T(128)} %param.20) | copy-start | bytes 388
  279.9 151.8 %copy-start.14 = (s32[1,512]{1,0:T(1,128)S(1)}, s32[1,512]{1,0:T(1,128)}, u32[]{:S(2)}) copy-start(s32[1,512]{1,0:T(1,128)} %param.18) | copy-start | bytes 6148
  279.9 237.2 %all-gather.4.cloned.1.call-start = ((), (), s32[]{:S(2)}) async-start(), calls=%async_computation.2 | async-start | bytes 1597440 | tf_op jit(solution)/shard_map/all_gather | solution.py:159
  428.9 92.2 %copy-start.3 = (bf16[8,1536]{1,0:T(8,128)(2,1)}, bf16[8,1536]{1,0:T(8,128)(2,1)S(1)}, u32[]{:S(2)}) copy-start(bf16[8,1536]{1,0:T(8,128)(2,1)S(1)} %get-tuple-element.250) | copy-start | bytes 73732
  521.1 282.0 %copy-start.6 = (s32[512]{0:T(512)S(1)}, s32[512]{0:T(512)}, u32[]{:S(2)}) copy-start(s32[512]{0:T(512)} %copy-done.5) | copy-start | bytes 6148
  (4 other events, 6.4 us)
Sparse Core Ops, SparseCore 0:
  11.3 89.9 all-gather.5
  280.0 147.9 reduce-scatter.1
  431.3 85.7 all-gather.3
where the time goes:
time: 821 us; the launch traced here: 820 us
  blocking collectives  427 us (52%)
  waiting for transfers between devices  314 us (38%)
  other arithmetic  22.4 us (3%)
  local copies, waits for them, and re-layouts  20.4 us (2%)
  matrix products  15.5 us (2%)
  between operations  14.9 us (2%)
    reduce_scatter x1, waiting for transfers between devices, shards(): lax.psum_scatter(jnp.dot(gated_norm, w_out, preferred_element_type=jnp.fl...  148 us
    psum x1, blocking collectives, shards(): expsum_all, target_all = lax.psum((expsum_local, target_local), 'blk')  142 us
    psum x1, blocking collectives, shards(): squares = lax.psum(jnp.sum(gated * gated, axis=1), 'blk')  138 us
    pmax x1, blocking collectives, shards(): top_all = lax.pmax(top_local, 'blk')  138 us
    all_gather x1, waiting for transfers between devices, shards(): lax.all_gather(final_norm(layer_own, final_gain), 'blk', axis=0, tiled=True)  85.4 us
    all_gather x1, waiting for transfers between devices, shards(): gathered = lax.all_gather(rows_own, 'blk', axis=0, tiled=True)  80.3 us
  transfers between devices with their start and end apart: 3, of which 3 were waited for; matrix products, arithmetic and copies ran while one was open for 2% of the time, Pallas kernels for 0%

commit v1 on v0

--- a/solution.py
+++ b/solution.py
@@ -156,7 +156,12 @@
     )
     layer_own = (rows_own.astype(jnp.float32) + delta_own).astype(jnp.bfloat16)
     logits = jnp.dot(
-        lax.all_gather(final_norm(layer_own, final_gain), "blk", axis=0, tiled=True),
+        jnp.concatenate(
+            lax.all_to_all(
+                jnp.stack([final_norm(layer_own, final_gain)] * lax.axis_size("blk")), "blk", 0, 0
+            ),
+            axis=0,
+        ),
         w_head,
         preferred_element_type=jnp.float32,
     )

time: 821 us -> 787 us (0.959)
  waiting for transfers between devices: 314 us -> 267 us
  starting transfers between devices: 0.12 us -> 13.8 us
    all_gather x1 -> x0, waiting for transfers between devices: 85.4 us -> none  [shards(): lax.all_gather(final_norm(layer_own, final_gain), 'blk', axis=0, tiled=True)]
    all_to_all x0 -> x1, waiting for transfers between devices: none -> 38.4 us  [shards(): lax.all_to_all(jnp.stack([final_norm(layer_own, final_gain)] * lax.axis_s...]
    all_to_all x0 -> x1, starting transfers between devices: none -> 13.7 us  [shards(): lax.all_to_all(jnp.stack([final_norm(layer_own, final_gain)] * lax.axis_s...]
where the time goes in v1:
time: 787 us; the launch traced here: 786 us
  blocking collectives  425 us (54%)
  waiting for transfers between devices  267 us (34%)
  local copies, waits for them, and re-layouts  21.7 us (3%)
  other arithmetic  21.7 us (3%)
  matrix products  15.5 us (2%)
  between operations  15.2 us (2%)
  starting transfers between devices  13.8 us (2%)
    reduce_scatter x1, waiting for transfers between devices, shards(): lax.psum_scatter(jnp.dot(gated_norm, w_out, preferred_element_type=jnp.fl...  148 us
    pmax x1, blocking collectives, shards(): top_all = lax.pmax(top_local, 'blk')  140 us
    psum x1, blocking collectives, shards(): expsum_all, target_all = lax.psum((expsum_local, target_local), 'blk')  139 us
    psum x1, blocking collectives, shards(): squares = lax.psum(jnp.sum(gated * gated, axis=1), 'blk')  138 us
    all_gather x1, waiting for transfers between devices, shards(): gathered = lax.all_gather(rows_own, 'blk', axis=0, tiled=True)  80.4 us
    all_to_all x1, waiting for transfers between devices, shards(): lax.all_to_all(jnp.stack([final_norm(layer_own, final_gain)] * lax.axis_s...  38.4 us
  transfers between devices with their start and end apart: 3, of which 3 were waited for; matrix products, arithmetic and copies ran while one was open for 2% of the time, Pallas kernels for 0%

profile of v1, /device:TPU:1, one launch (start us, length us, event | category | flops | bytes accessed | tf_op | source)
XLA Modules:
  0.0 785.6 jit_solution(2286627886554938423)
XLA Ops:
  10.2 1.4 gather_fusion
  13.6 1.4 slice_bitcast_fusion.3
  15.0 4.3 compare_select_fusion.5
  20.9 80.4 %all-gather.3.cloned.1.call-done = bf16[1,512,1536]{2,1,0:T(8,128)(2,1)} async-done(((bf16[1,8,1536]{2,1,0:T(8,128)(2,1)}), bf16[1,512,1536]{2,1,0:T(8,128)(2,1)}) %all-gather.3.cloned.1.call-update) | async-done | bytes 1572880 | tf_op jit(solution)/shard_map/all_gather | solution.py:62
  101.3 2.3 fusion.73
  104.8 2.0 fusion.76
  108.1 29.2 %while.17 = (s32[]{:T(128)}, f32[48,128]{1,0:T(8,128)S(1)}, s32[]{:T(128)}, f32[2,256,48]{1,0,2:T(2,128)}, s32[2,256]{1,0:T(2,128)}, /*index=5*/f32[2,256,2]{1,2...) while((s32[]{:T(128)}, f32[48,128]{1,0:T(8,128)S(1)}, ...), condition=%wide.region_5.6_spmd.clone.clone.clone, body=%wide.region_2.5_spmd.clone.clone.clone.sunk | while | flops 215140816 | bytes 2177448 | solution.py:145
  113.8 1.3 constant_dynamic-slice_fusion.12
  115.1 2.0 compare_convert_fusion.10
  118.0 2.2 dynamic_update_slice.8
  128.3 1.3 constant_dynamic-slice_fusion.12
  129.6 2.0 compare_convert_fusion.10
  132.6 2.2 dynamic_update_slice.8
  138.8 138.1 %psum.21 = f32[512]{0:T(512)S(1)} all-reduce(f32[512]{0:T(512)S(1)} %get-tuple-element.251), channel_id=1, replica_groups=mesh['blk'=64,'seq'=4,'mp'=2] {'blk'}, use_global_device_ids=true, to_apply=%region_7.8 | all-reduce | flops 512 | bytes 4096 | tf_op jit(solution)/shard_map/psum | solution.py:148
  276.9 3.0 fusion.87
  279.9 147.8 %reduce-scatter.2.cloned.1.call-done = f32[8,1536]{1,0:T(8,128)} async-done(((f32[512,1536]{1,0:T(8,128)}), f32[8,1536]{1,0:T(8,128)}) %reduce-scatter.2.cloned.1.call-update) | async-done | bytes 49168 | tf_op jit(solution)/shard_map/reduce_scatter | solution.py:151
  428.8 1.3 stack.2
  430.1 13.7 %all-to-all-start = ((bf16[64,8,1536]{2,1,0:T(8,128)(2,1)}), bf16[64,8,1536]{2,1,0:T(8,128)(2,1)}, u32[]{:S(2)}, u32[]{:S(2)}) async-start(bf16[64,8,1536]{2,1,0:T(8,128)(2,1)} %stack.2), calls=%async_computation.1 | async-start | bytes 3145728 | tf_op jit(solution)/shard_map/all_to_all | solution.py:160
  445.9 38.4 %all-to-all-done = bf16[64,8,1536]{2,1,0:T(8,128)(2,1)} async-done(((bf16[64,8,1536]{2,1,0:T(8,128)(2,1)}), bf16[64,8,1536]{2,1,0:T(8,128)(2,1)}, u32[]{:S(2)}, u32[]{:S(2)}) %all-to-all-start) | async-done | bytes 1572896 | tf_op jit(solution)/shard_map/all_to_all | solution.py:160
  484.3 4.0 fusion.103
  488.3 139.6 %pmax.7 = f32[512]{0:T(512)S(1)} all-reduce(f32[512]{0:T(512)S(1)} %get-tuple-element.299), channel_id=1, replica_groups=mesh['blk'=64,'seq'=4,'mp'=2] {'blk'}, use_global_device_ids=true, to_apply=%region_13.14 | all-reduce | flops 512 | bytes 4096 | tf_op jit(solution)/shard_map/pmax | solution.py:173
  627.8 1.9 exponential_reduce_fusion
  629.7 139.0 %all-reduce.7 = (f32[512]{0:T(512)S(1)}, f32[512]{0:T(512)S(1)}) all-reduce(f32[512]{0:T(512)S(1)} %get-tuple-element.222, f32[512]{0:T(512)S(1)} %get-tuple-element.221), channel_id=1, replica_groups=mesh['blk'=64,'seq'=4,'mp'=2] {'blk'}, use_global_device_ids=true, to_apply=%region_11.12 | all-reduce | flops 1024 | bytes 8192 | tf_op jit(solution)/shard_map/psum | solution.py:175
  769.2 8.4 %all-reduce.6 = f32[32]{0:T(128)S(1)} all-reduce(f32[32]{0:T(128)S(1)} %convolution_bitcast_fusion.1), channel_id=4, replica_groups=mesh['blk'=64,'seq'=4,'mp'=2] {'seq'}, use_global_device_ids=true, to_apply=%region_16.17.clone | all-reduce | flops 32 | bytes 256
  (135 shorter events, 27.1 us)
Async XLA Ops:
  7.2 477.1 %copy-start = (bf16[1536,786]{0,1:T(8,128)(2,1)S(1)}, bf16[1536,786]{0,1:T(8,128)(2,1)}, u32[]{:S(2)}) copy-start(bf16[1536,786]{0,1:T(8,128)(2,1)} %param.31) | copy-start | bytes 7243780
  7.2 94.1 %all-gather.3.cloned.1.call-start = ((), (), s32[]{:S(2)}) async-start(), calls=%async_computation.3 | async-start | bytes 1597440 | tf_op jit(solution)/shard_map/all_gather | solution.py:62
  7.9 419.9 %reduce-scatter.2.cloned.1.call-start = ((), (), s32[]{:S(2)}) async-start(), calls=%async_computation.2 | async-start | bytes 3194880 | tf_op jit(solution)/shard_map/reduce_scatter | solution.py:151
  9.6 94.1 %copy-start.5 = (s32[512]{0:T(512)}, s32[512]{0:T(512)S(1)}, u32[]{:S(2)}) copy-start(s32[512]{0:T(512)S(1)} %get-tuple-element.290) | copy-start | bytes 6148
  20.0 83.7 %copy-start.11 = (f32[512]{0:T(512)}, f32[512]{0:T(512)S(1)}, u32[]{:S(2)}) copy-start(f32[512]{0:T(512)S(1)} %get-tuple-element.257) | copy-start | bytes 6148
  20.0 83.7 %copy-start.7 = (f32[512]{0:T(512)}, f32[512]{0:T(512)S(1)}, u32[]{:S(2)}) copy-start(f32[512]{0:T(512)S(1)} %get-tuple-element.287) | copy-start | bytes 6148
  20.1 83.7 %copy-start.9 = (f32[512]{0:T(512)}, f32[512]{0:T(512)S(1)}, u32[]{:S(2)}) copy-start(f32[512]{0:T(512)S(1)} %get-tuple-element.288) | copy-start | bytes 6148
  104.7 2.2 copy-start.21
  104.8 2.3 copy-start.8
  104.8 2.3 copy-start.10
  104.8 2.3 copy-start.12
  104.8 2.3 copy-start.15
  104.8 2.3 copy-start.16
  104.8 2.3 copy-start.17
  104.8 2.3 copy-start.18
  104.8 2.3 copy-start.19
  104.8 2.3 copy-start.20
  108.1 168.9 %copy-start.1 = (bf16[48,1536]{1,0:T(8,128)(2,1)S(1)}, bf16[48,1536]{1,0:T(8,128)(2,1)}, u32[]{:S(2)}) copy-start(bf16[48,1536]{1,0:T(8,128)(2,1)} %param.29) | copy-start | bytes 442372
  279.9 147.8 %copy-start.4 = (bf16[1,8,1536]{2,1,0:T(8,128)(2,1)S(1)}, bf16[1,8,1536]{2,1,0:T(8,128)(2,1)}, u32[]{:S(2)}) copy-start(bf16[1,8,1536]{2,1,0:T(8,128)(2,1)} %param.17) | copy-start | bytes 73732
  279.9 148.8 %copy-start.13 = (f32[1536]{0:T(1024)S(1)}, f32[1536]{0:T(1024)}, u32[]{:S(2)}) copy-start(f32[1536]{0:T(1024)} %param.30) | copy-start | bytes 18436
  430.1 13.8 %copy-start.23 = (s32[32]{0:T(128)S(1)}, s32[32]{0:T(128)}, u32[]{:S(2)}) copy-start(s32[32]{0:T(128)} %param.20) | copy-start | bytes 388
  430.1 15.8 %copy-start.14 = (s32[1,512]{1,0:T(1,128)S(1)}, s32[1,512]{1,0:T(1,128)}, u32[]{:S(2)}) copy-start(s32[1,512]{1,0:T(1,128)} %param.18) | copy-start | bytes 6148
  430.1 54.2 %all-to-all-start = ((bf16[64,8,1536]{2,1,0:T(8,128)(2,1)}), bf16[64,8,1536]{2,1,0:T(8,128)(2,1)}, u32[]{:S(2)}, u32[]{:S(2)}) async-start(bf16[64,8,1536]{2,1,0:T(8,128)(2,1)} %stack.2), calls=%async_computation.1 | async-start | bytes 3145728 | tf_op jit(solution)/shard_map/all_to_all | solution.py:160
  488.3 280.4 %copy-start.6 = (s32[512]{0:T(512)S(1)}, s32[512]{0:T(512)}, u32[]{:S(2)}) copy-start(s32[512]{0:T(512)} %copy-done.5) | copy-start | bytes 6148
  (4 other events, 5.6 us)
Sparse Core Ops, SparseCore 0:
  11.3 89.9 all-gather.2
  280.1 147.6 reduce-scatter.1
